TPU v7x, 256 devices: a whole 4x4x8 slice. The times are simulated.
256 devices in a mesh: lon: 64 (over y, z, x_hi), lat: 4 (over x_lo, core).
Axes of the slice: x: 4 (x_hi: 2, x_lo: 2; x = x_hi * 2 + x_lo), y: 4, z: 8, core: 2. Of those that a mesh axis runs over, the one named last changes fastest.
Arguments:
- initial_state: float32 [4, 32, 1024, 512], P(None, None, 'lon', 'lat'), may hold values from -6 to 6
- coefficients: float32 [4, 32, 1024, 512], P(None, None, 'lon', 'lat'), may hold values from 0.02 to 0.24
- coupling: float32 [32, 4, 4], replicated, may hold values from -3 to 3
- obs_band: int32 [4, 32768, 1], P('lat', 'lon'), may hold values from 0 to 63; in each aligned block of 512 rows (0 to 511, 512 to 1023, ..., all dimensions but the last counted through in order) at most 32 rows name the same one
- obs_cell: int32 [4, 32768], P('lat', 'lon'), may hold values from 0 to 262143
- obs_value: float32 [4, 32768], P('lat', 'lon'), may hold values from -6 to 6
- obs_weight: float32 [4, 32768], P('lat', 'lon'), may hold values from 0.5 to 4
- obs_count: int32 [4, 64], P('lat', 'lon'), may hold values from 256 to 512
Outputs:
- final_state: float32 [4, 32, 1024, 512], P(None, None, 'lon', 'lat')
- gradient: float32 [4, 32, 1024, 512], P(None, None, 'lon', 'lat')
Inputs may be any that keep to these rules, and one draw needn't show every extreme that they name: `obs_band`: in the 512 rows of one device no band is named more than 32 times, a bound that some block reaches.
All inputs are finite; a program needn't handle non-finite values.
Results may differ from a plain program's by a relative error of at most 0.0003.
Values sent between devices are 32-bit elements; how exact they have to be, the bound alone decides.
No kernel may reach another device: no remote copies, remote signals or barrier semaphores. Data moves between devices by JAX's collectives and lax.ppermute only.
A program may use at most 128 MiB of HBM per device.

v0:
```python
import jax
import jax.numpy as jnp
from jax import lax
from jax.sharding import PartitionSpec as P

STEPS = 2


def extended(array, sides, width, wrap):
    for axis, dim in sides:
        peers, length = (lax.axis_size(axis), array.shape[dim])
        up = [(i, (i + 1) % peers) for i in range(peers if wrap else peers - 1)]
        down = [(j, i) for i, j in up]
        last = lax.slice_in_dim(array, length - width, length, axis=dim)
        initial = lax.slice_in_dim(array, 0, width, axis=dim)
        before = lax.ppermute(last, axis, up)
        after = lax.ppermute(initial, axis, down)
        array = jnp.concatenate([before, array, after], axis=dim)
    return array


def passed_along(value, axis, steps):
    count = lax.axis_size(axis)
    pairs = [(source, (source + steps) % count) for source in range(count)]
    return lax.ppermute(value, axis, pairs)


def neighbours(field, flip):
    ext_lon = extended(field, (("lon", 2),), 1, True)
    ext_lat = extended(field, (("lat", 3),), 1, False)
    west = ext_lon[:, :, :-2, :]
    east = ext_lon[:, :, 2:, :]
    north = ext_lat[:, :, :, :-2]
    south = ext_lat[:, :, :, 2:]
    edges = jnp.stack([field[:, :, :, 0], field[:, :, :, -1]])
    partner = passed_along(edges, "lon", lax.axis_size("lon") // 2)
    position = lax.axis_index("lat")
    last_block = lax.axis_size("lat") - 1
    north = north.at[:, :, :, 0].set(jnp.where(position == 0, flip * partner[0], north[:, :, :, 0]))
    south = south.at[:, :, :, -1].set(
        jnp.where(position == last_block, flip * partner[1], south[:, :, :, -1])
    )
    return (north, south, west, east)


def on_device(
    initial_state, coefficients, coupling, obs_band, obs_cell, obs_value, obs_weight, obs_count
):
    wind_flip = jnp.array([-1.0, -1.0, 1.0, 1.0], dtype=jnp.float32).reshape(4, 1, 1)
    plain_flip = jnp.ones((4, 1, 1), jnp.float32)
    total = coefficients[0] + coefficients[1] + coefficients[2] + coefficients[3]
    stored = []
    x = initial_state
    for step in range(STEPS):
        forward_north, forward_south, forward_west, forward_east = neighbours(x, wind_flip)
        mixed = jnp.einsum("lgf,flij->glij", coupling, x, precision=lax.Precision.HIGHEST)
        y = (
            x
            + coefficients[0] * forward_north
            + coefficients[1] * forward_south
            + coefficients[2] * forward_west
            + coefficients[3] * forward_east
            - total * x
            + 0.25 * mixed
        )
        stored.append(y)
        x = y - 0.5 * jnp.tanh(y)
    rows = obs_cell.shape[1]
    band = obs_band[0, :, 0]
    valid = jnp.arange(rows, dtype=jnp.int32) < obs_count[0, 0]
    weight = jnp.where(valid, obs_weight[0], 0.0)
    cell_float = obs_cell[0].astype(jnp.float32)
    payload = jnp.stack([obs_value[0], weight, cell_float, band.astype(jnp.float32)])
    arrived = lax.all_gather(payload, "lon", axis=1, tiled=True)
    owned = (arrived[3] == lax.axis_index("lon").astype(jnp.float32)).astype(jnp.float32)
    values = arrived[0]
    weights = arrived[1] * owned
    cells = arrived[2].astype(jnp.int32)
    flat_state = x.reshape(-1)
    forcing = weights * (flat_state[cells] - values)
    lam = jnp.zeros_like(flat_state).at[cells].add(forcing).reshape(x.shape)
    near_n, near_s, near_w, near_e = neighbours(coefficients, plain_flip)
    row_ids = jnp.arange(coefficients.shape[3], dtype=jnp.int32)[None, :]
    polar_top = (lax.axis_index("lat") == 0) & (row_ids == 0)
    polar_bottom = (lax.axis_index("lat") == lax.axis_size("lat") - 1) & (
        row_ids == coefficients.shape[3] - 1
    )
    from_north = jnp.where(polar_top, near_n[0], near_n[1])
    from_south = jnp.where(polar_bottom, near_s[1], near_s[0])
    from_west = near_w[3]
    from_east = near_e[2]
    for step in range(STEPS - 1, -1, -1):
        squashed = jnp.tanh(stored[step])
        lam_y = lam * (1.0 - 0.5 * (1.0 - squashed * squashed))
        north, south, west, east = neighbours(lam_y, wind_flip)
        back = jnp.einsum("lgf,glij->flij", coupling, lam_y, precision=lax.Precision.HIGHEST)
        lam = (
            lam_y
            - total * lam_y
            + 0.25 * back
            + from_north * north
            + from_south * south
            + from_west * west
            + from_east * east
        )
    return (x, lam)


def solution(mesh):
    in_specs = (
        P(None, None, "lon", "lat"),
        P(None, None, "lon", "lat"),
        P(),
        P("lat", "lon", None),
        P("lat", "lon"),
        P("lat", "lon"),
        P("lat", "lon"),
        P("lat", "lon"),
    )
    out_specs = (P(None, None, "lon", "lat"), P(None, None, "lon", "lat"))
    return jax.shard_map(
        on_device, mesh=mesh, in_specs=in_specs, out_specs=out_specs, check_vma=False
    )
```

profile of v0, /device:TPU:1, one launch (start us, length us, event | category | flops | bytes accessed | tf_op | source)
XLA Modules:
  0.0 978.5 jit_solution(12267966740924993856)
XLA Ops:
  0.6 1.9 fusion.37
  2.6 3.6 collective-permute-start.16
  6.1 2.0 fusion.42
  9.2 3.1 collective-permute-start
  13.4 1.9 collective-permute-start.2
  16.6 2.4 copy.769
  19.0 3.6 collective-permute-start.10
  23.8 1.9 collective-permute-start.14
  30.8 157.5 %all_gather.3 = f32[4,32768]{1,0:T(4,128)S(1)} all-gather(f32[4,512]{1,0:T(4,128)S(1)} %pad_maximum_fusion.25), channel_id=1, replica_groups=mesh['lon'=64,'lat'=4] {'lon'}, dimensions={1}, use_global_device_ids=true | all-gather | bytes 532480 | tf_op jit(solution)/shard_map/all_gather | solution.py:74
  193.1 1.9 copy.691
  195.1 1.9 copy.698
  197.1 4.6 pad_maximum_fusion.17
  201.6 3.0 collective-permute-start.3
  204.6 2.2 copy.723
  206.8 10.1 %collective-permute-start.1 = (f32[2,4,32,16]{2,3,1,0:T(8,128)}, f32[2,4,32,16]{2,3,1,0:T(8,128)}, u32[]{:S(2)}, u32[]{:S(2)}) collective-permute-start(f32[2,4,32,16]{2,3,1,0:T(8,128)} %pad_maximum_fusion.20), channel_id=1, source_target_pairs={{0,128},{4,132},{8,136},{12,140},{16,144},{20,148},{24,152},{28,15... | collective-permute-start | bytes 49160 | tf_op jit(solution)/shard_map/ppermute | solution.py:25
  216.9 2.2 copy.734
  219.1 3.7 pad_maximum_fusion.9
  222.9 2.6 copy.736
  225.5 2.6 copy.726
  228.1 3.0 collective-permute-start.11
  232.4 2.6 copy.694
  235.0 2.6 copy.699
  239.0 2.7 copy.735
  244.2 2.7 copy.725
  249.3 4.0 scatter.40
  253.3 3.8 multiply_select_fusion.7
  257.1 12.0 %scatter.44 = f32[4,32,16,128]{3,2,1,0:T(8,128)} dynamic-update-slice(f32[4,32,16,128]{3,2,1,0:T(8,128)} %get-tuple-element.157, f32[4,32,16,1]{3,2,1,0:T(8,128)} %copy.737, s32[]{:T(128)} %constant.234.clone.1, s32[]{:T(128)} %constant.234.clone.1, s32[]{:T(128)} %constant.234.clone.1, s32[]{:T(128)} %constant.236.clone.1) | dynamic-update-slice | bytes 16388 | tf_op jit(solution)/shard_map/scatter | solution.py:40
  269.1 2.0 fusion.31
  271.1 43.3 %scatter.35 = f32[4,32,16,128]{3,0,2,1:T(4,128)} dynamic-update-slice(f32[4,32,16,128]{3,0,2,1:T(4,128)} %get-tuple-element.182, f32[4,32,16,1]{3,0,2,1:T(4,128)S(1)} %copy-done.6, s32[]{:T(128)} %constant.234.clone.1, s32[]{:T(128)} %constant.234.clone.1, s32[]{:T(128)} %constant.234.clone.1, s32[]{:T(128)} %constant.236.clone.1) | dynamic-update-slice | bytes 16388 | tf_op jit(solution)/shard_map/scatter | solution.py:40
  314.4 8.9 scatter.34
  323.3 1.9 fusion.30
  325.3 5.2 multiply_subtract_fusion.3
  331.8 4.3 collective-permute-start.9
  337.4 32.4 %collective-permute-start.5 = (f32[4,32,16,1]{1,2,3,0:T(8,128)}, f32[4,32,16,1]{1,2,3,0:T(8,128)S(1)}, u32[]{:S(2)}, u32[]{:S(2)}) collective-permute-start(f32[4,32,16,1]{1,2,3,0:T(8,128)} %copy.708), channel_id=1, source_target_pairs={{0,1},{1,2},{2,3},{4,5},{5,6},{6,7},{8,9},{9,10},{10,11},{12,13},{... | collective-permute-start | bytes 24584 | tf_op jit(solution)/shard_map/ppermute | solution.py:16
  370.4 1.9 collective-permute-start.7
  375.7 1.9 copy.715
  377.7 3.0 pad_maximum_fusion.13
  382.1 2.6 copy.712
  384.7 2.6 copy.716
  387.2 3.8 multiply_select_fusion.5
  391.0 43.3 %scatter.39 = f32[4,32,16,128]{3,0,2,1:T(4,128)} dynamic-update-slice(f32[4,32,16,128]{3,0,2,1:T(4,128)} %get-tuple-element.176, f32[4,32,16,1]{3,0,2,1:T(4,128)} %get-tuple-element.204, s32[]{:T(128)} %constant.234.clone.1, s32[]{:T(128)} %constant.234.clone.1, s32[]{:T(128)} %constant.234.clone.1, s32[]{:T(128)} %constant.236.clone.1) | dynamic-update-slice | bytes 16388 | tf_op jit(solution)/shard_map/scatter | solution.py:40
  434.3 8.0 scatter.36
  442.3 5.9 multiply_subtract_fusion.2
  449.2 180.5 %gather_fusion = f32[32768]{0:T(1024)S(1)} fusion(f32[262144]{0:T(1024)S(1)} %bitcast.99, s32[32768]{0:T(1024)S(1)} %copy-done.17), kind=kCustom, calls=%fused_computation | custom fusion | bytes 393216 | tf_op jit(solution)/shard_map/gather | solution.py:80
  629.8 171.5 %scatter_custom_fusion = f32[262144]{0:T(1024)S(1)} fusion(s32[32768]{0:T(1024)S(1)} %bitcast.108, f32[32768]{0:T(1024)S(1)} %subtract_multiply_fusion, f32[]{:T(128)} %constant.239.clone.1), kind=kCustom, calls=%fused_computation.65 | custom fusion | flops 32768 | bytes 1048580 | tf_op jit(solution)/shard_map/scatter-add | solution.py:81
  803.5 8.1 collective-permute-start.19
  812.2 1.9 collective-permute-start.12
  814.8 2.4 collective-permute-start.15
  817.2 2.1 collective-permute-start.13
  821.6 3.0 pad_maximum_fusion.8
  828.3 3.8 multiply_select_fusion.3
  832.1 43.3 %scatter.45 = f32[4,32,16,128]{3,0,2,1:T(4,128)} dynamic-update-slice(f32[4,32,16,128]{3,0,2,1:T(4,128)} %get-tuple-element.170, f32[4,32,16,1]{3,0,2,1:T(4,128)} %get-tuple-element.202, s32[]{:T(128)} %constant.234.clone.1, s32[]{:T(128)} %constant.234.clone.1, s32[]{:T(128)} %constant.234.clone.1, s32[]{:T(128)} %constant.236.clone.1) | dynamic-update-slice | bytes 16388 | tf_op jit(solution)/shard_map/scatter | solution.py:40
  875.4 8.0 scatter.41
  883.5 4.9 fusion.12
  889.7 7.5 collective-permute-start.24
  898.1 3.6 collective-permute-start.20
  902.4 1.9 collective-permute-start.22
  908.0 1.9 copy.750
  909.9 3.0 pad_maximum_fusion.3
  913.7 1.8 copy.747
  917.4 3.8 multiply_select_fusion.1
  921.1 43.3 %scatter.49 = f32[4,32,16,128]{3,0,2,1:T(4,128)} dynamic-update-slice(f32[4,32,16,128]{3,0,2,1:T(4,128)} %get-tuple-element.151, f32[4,32,16,1]{3,0,2,1:T(4,128)} %get-tuple-element.200, s32[]{:T(128)} %constant.234.clone.1, s32[]{:T(128)} %constant.234.clone.1, s32[]{:T(128)} %constant.234.clone.1, s32[]{:T(128)} %constant.236.clone.1) | dynamic-update-slice | bytes 16388 | tf_op jit(solution)/shard_map/scatter | solution.py:40
  964.5 8.0 scatter.46
  972.5 4.6 fusion.7
  (151 shorter events, 50.4 us)
Async XLA Ops:
  2.6 320.7 %collective-permute-start.16 = (f32[4,32,1,128]{3,2,1,0:T(1,128)}, f32[4,32,1,128]{3,2,1,0:T(1,128)}, u32[]{:S(2)}, u32[]{:S(2)}) collective-permute-start(f32[4,32,1,128]{3,2,1,0:T(1,128)} %get-tuple-element.167), channel_id=1, source_target_pairs={{0,4},{4,8},{8,12},{12,16},{16,20},{20,24},{24,28},{28,32},{32,36}... | collective-permute-start | bytes 196616 | tf_op jit(solution)/shard_map/ppermute | solution.py:16
  8.1 7.2 copy-start.1
  9.2 183.9 %collective-permute-start = (f32[4,32,16,1]{1,2,3,0:T(8,128)}, f32[4,32,16,1]{1,2,3,0:T(8,128)}, u32[]{:S(2)}, u32[]{:S(2)}) collective-permute-start(f32[4,32,16,1]{1,2,3,0:T(8,128)} %copy.767), channel_id=1, source_target_pairs={{0,1},{1,2},{2,3},{4,5},{5,6},{6,7},{8,9},{9,10},{10,11},{12,13},{... | collective-permute-start | bytes 24584 | tf_op jit(solution)/shard_map/ppermute | solution.py:16
  13.4 181.7 %collective-permute-start.2 = (f32[4,32,16,1]{1,2,3,0:T(8,128)}, f32[4,32,16,1]{1,2,3,0:T(8,128)}, u32[]{:S(2)}, u32[]{:S(2)}) collective-permute-start(f32[4,32,16,1]{1,2,3,0:T(8,128)} %copy.768), channel_id=1, source_target_pairs={{1,0},{2,1},{3,2},{5,4},{6,5},{7,6},{9,8},{10,9},{11,10},{13,12},{... | collective-permute-start | bytes 24584 | tf_op jit(solution)/shard_map/ppermute | solution.py:17
  16.6 9.0 copy-start.2
  19.0 182.6 %collective-permute-start.10 = (f32[4,32,16,1]{1,2,3,0:T(8,128)}, f32[4,32,16,1]{1,2,3,0:T(8,128)}, u32[]{:S(2)}, u32[]{:S(2)}) collective-permute-start(f32[4,32,16,1]{1,2,3,0:T(8,128)} %copy.769), channel_id=1, source_target_pairs={{0,1},{1,2},{2,3},{4,5},{5,6},{6,7},{8,9},{9,10},{10,11},{12,13},{... | collective-permute-start | bytes 24584 | tf_op jit(solution)/shard_map/ppermute | solution.py:16
  23.8 183.0 %collective-permute-start.14 = (f32[4,32,16,1]{1,2,3,0:T(8,128)}, f32[4,32,16,1]{1,2,3,0:T(8,128)}, u32[]{:S(2)}, u32[]{:S(2)}) collective-permute-start(f32[4,32,16,1]{1,2,3,0:T(8,128)} %copy.770), channel_id=1, source_target_pairs={{1,0},{2,1},{3,2},{5,4},{6,5},{7,6},{9,8},{10,9},{11,10},{13,12},{... | collective-permute-start | bytes 24584 | tf_op jit(solution)/shard_map/ppermute | solution.py:17
  26.4 1.0 copy-start.3
  28.0 0.7 copy-start.29
  28.7 0.7 copy-start.30
  29.4 0.7 copy-start.31
  30.1 0.7 copy-start.32
  189.5 2.8 copy-start.28
  193.1 130.2 %collective-permute-start.18 = (f32[4,32,1,128]{3,2,1,0:T(1,128)}, f32[4,32,1,128]{3,2,1,0:T(1,128)}, u32[]{:S(2)}, u32[]{:S(2)}) collective-permute-start(f32[4,32,1,128]{3,2,1,0:T(1,128)} %get-tuple-element.168), channel_id=1, source_target_pairs={{4,0},{8,4},{12,8},{16,12},{20,16},{24,20},{28,24},{32,28},{36,32}... | collective-permute-start | bytes 196616 | tf_op jit(solution)/shard_map/ppermute | solution.py:17
  195.0 130.2 %collective-permute-start.4 = (f32[4,32,1,128]{3,0,2,1:T(4,128)}, f32[4,32,1,128]{3,0,2,1:T(4,128)}, u32[]{:S(2)}, u32[]{:S(2)}) collective-permute-start(f32[4,32,1,128]{3,0,2,1:T(4,128)} %get-tuple-element.186), channel_id=1, source_target_pairs={{4,0},{8,4},{12,8},{16,12},{20,16},{24,20},{28,24},{32,28},{36,32}... | collective-permute-start | bytes 196616 | tf_op jit(solution)/shard_map/ppermute | solution.py:17
  201.6 123.6 %collective-permute-start.3 = (f32[4,32,1,128]{3,0,2,1:T(4,128)}, f32[4,32,1,128]{3,0,2,1:T(4,128)}, u32[]{:S(2)}, u32[]{:S(2)}) collective-permute-start(f32[4,32,1,128]{3,0,2,1:T(4,128)} %get-tuple-element.185), channel_id=1, source_target_pairs={{0,4},{4,8},{8,12},{12,16},{16,20},{20,24},{24,28},{28,32},{32,36}... | collective-permute-start | bytes 196616 | tf_op jit(solution)/shard_map/ppermute | solution.py:16
  206.8 21.3 %collective-permute-start.1 = (f32[2,4,32,16]{2,3,1,0:T(8,128)}, f32[2,4,32,16]{2,3,1,0:T(8,128)}, u32[]{:S(2)}, u32[]{:S(2)}) collective-permute-start(f32[2,4,32,16]{2,3,1,0:T(8,128)} %pad_maximum_fusion.20), channel_id=1, source_target_pairs={{0,128},{4,132},{8,136},{12,140},{16,144},{20,148},{24,152},{28,15... | collective-permute-start | bytes 49160 | tf_op jit(solution)/shard_map/ppermute | solution.py:25
  228.1 9.5 collective-permute-start.11
  249.3 4.0 copy-start.27
  257.1 12.0 %copy-start.10 = (f32[4,32,16,128]{3,2,1,0:T(8,128)S(1)}, f32[4,32,16,128]{3,2,1,0:T(8,128)}, u32[]{:S(2)}) copy-start(f32[4,32,16,128]{3,2,1,0:T(8,128)} %scatter.40) | copy-start | bytes 3145732
  269.1 2.0 copy-start.6
  271.1 43.3 %copy-start.5 = (f32[4,32,16,1]{3,0,2,1:T(4,128)S(1)}, f32[4,32,16,1]{3,0,2,1:T(4,128)}, u32[]{:S(2)}) copy-start(f32[4,32,16,1]{3,0,2,1:T(4,128)} %get-tuple-element.205) | copy-start | bytes 24580
  323.3 2.0 copy-start.4
  323.3 2.0 copy-start.11
  323.3 2.0 copy-start.12
  323.3 2.0 copy-start.25
  325.2 5.2 copy-start.19
  325.2 5.2 copy-start.20
  325.2 5.2 copy-start.21
  325.2 5.2 copy-start.22
  325.2 5.3 copy-start.23
  331.8 110.5 %collective-permute-start.9 = (f32[4,32,1,128]{3,0,2,1:T(4,128)}, f32[4,32,1,128]{3,0,2,1:T(4,128)}, u32[]{:S(2)}, u32[]{:S(2)}) collective-permute-start(f32[4,32,1,128]{3,0,2,1:T(4,128)} %get-tuple-element.180), channel_id=1, source_target_pairs={{4,0},{8,4},{12,8},{16,12},{20,16},{24,20},{28,24},{32,28},{36,32}... | collective-permute-start | bytes 196616 | tf_op jit(solution)/shard_map/ppermute | solution.py:17
  336.1 106.2 %collective-permute-start.8 = (f32[4,32,1,128]{3,0,2,1:T(4,128)}, f32[4,32,1,128]{3,0,2,1:T(4,128)}, u32[]{:S(2)}, u32[]{:S(2)}) collective-permute-start(f32[4,32,1,128]{3,0,2,1:T(4,128)} %get-tuple-element.179), channel_id=1, source_target_pairs={{0,4},{4,8},{8,12},{12,16},{16,20},{20,24},{24,28},{28,32},{32,36}... | collective-permute-start | bytes 196616 | tf_op jit(solution)/shard_map/ppermute | solution.py:16
  337.4 35.6 %collective-permute-start.5 = (f32[4,32,16,1]{1,2,3,0:T(8,128)}, f32[4,32,16,1]{1,2,3,0:T(8,128)S(1)}, u32[]{:S(2)}, u32[]{:S(2)}) collective-permute-start(f32[4,32,16,1]{1,2,3,0:T(8,128)} %copy.708), channel_id=1, source_target_pairs={{0,1},{1,2},{2,3},{4,5},{5,6},{6,7},{8,9},{9,10},{10,11},{12,13},{... | collective-permute-start | bytes 24584 | tf_op jit(solution)/shard_map/ppermute | solution.py:16
  369.7 2.6 copy-start.24
  370.4 5.3 collective-permute-start.7
  373.0 7.7 collective-permute-start.6
  391.0 43.3 %copy-start.8 = (f32[4,32,16,1]{3,0,2,1:T(4,128)S(1)}, f32[4,32,16,1]{3,0,2,1:T(4,128)}, u32[]{:S(2)}) copy-start(f32[4,32,16,1]{3,0,2,1:T(4,128)} %get-tuple-element.203) | copy-start | bytes 24580
  391.0 43.3 %copy-start.14 = (f32[4,32,16,128]{3,0,2,1:T(4,128)S(1)}, f32[4,32,16,128]{3,0,2,1:T(4,128)}, u32[]{:S(2)}) copy-start(f32[4,32,16,128]{3,0,2,1:T(4,128)} %get-tuple-element.175) | copy-start | bytes 3145732
  448.3 0.9 copy-start.17
  448.4 181.4 %copy-start = (f32[4,32,16,128]{3,2,1,0:T(8,128)}, f32[4,32,16,128]{3,2,1,0:T(8,128)S(1)}, u32[]{:S(2)}) copy-start(f32[4,32,16,128]{3,2,1,0:T(8,128)S(1)} %copy.753) | copy-start | bytes 3145732
  629.7 171.5 %copy-start.16 = (f32[4,32,16,128]{3,0,2,1:T(4,128)S(1)}, f32[4,32,16,128]{3,0,2,1:T(4,128)}, u32[]{:S(2)}) copy-start(f32[4,32,16,128]{3,0,2,1:T(4,128)} %get-tuple-element.210) | copy-start | bytes 3145732
  803.5 80.0 %collective-permute-start.19 = (f32[4,32,1,128]{3,0,2,1:T(4,128)}, f32[4,32,1,128]{3,0,2,1:T(4,128)}, u32[]{:S(2)}, u32[]{:S(2)}) collective-permute-start(f32[4,32,1,128]{3,0,2,1:T(4,128)} %get-tuple-element.174), channel_id=1, source_target_pairs={{4,0},{8,4},{12,8},{16,12},{20,16},{24,20},{28,24},{32,28},{36,32}... | collective-permute-start | bytes 196616 | tf_op jit(solution)/shard_map/ppermute | solution.py:17
  811.5 71.9 %collective-permute-start.17 = (f32[4,32,1,128]{3,0,2,1:T(4,128)S(1)}, f32[4,32,1,128]{3,0,2,1:T(4,128)}, u32[]{:S(2)}, u32[]{:S(2)}) collective-permute-start(f32[4,32,1,128]{3,0,2,1:T(4,128)S(1)} %get-tuple-element.173), channel_id=1, source_target_pairs={{0,4},{4,8},{8,12},{12,16},{16,20},{20,24},{24,28},{28,32},{32,36}... | collective-permute-start | bytes 196616 | tf_op jit(solution)/shard_map/ppermute | solution.py:16
  812.2 7.1 collective-permute-start.12
  814.8 5.7 collective-permute-start.15
  817.2 7.4 collective-permute-start.13
  832.1 43.3 %copy-start.9 = (f32[4,32,16,1]{3,0,2,1:T(4,128)S(1)}, f32[4,32,16,1]{3,0,2,1:T(4,128)}, u32[]{:S(2)}) copy-start(f32[4,32,16,1]{3,0,2,1:T(4,128)} %get-tuple-element.201) | copy-start | bytes 24580
  832.1 43.3 %copy-start.15 = (f32[4,32,16,128]{3,0,2,1:T(4,128)S(1)}, f32[4,32,16,128]{3,0,2,1:T(4,128)}, u32[]{:S(2)}) copy-start(f32[4,32,16,128]{3,0,2,1:T(4,128)} %get-tuple-element.169) | copy-start | bytes 3145732
  875.4 8.0 copy-start.18
  875.4 8.0 copy-start.26
  889.7 82.7 %collective-permute-start.24 = (f32[4,32,1,128]{3,0,2,1:T(4,128)}, f32[4,32,1,128]{3,0,2,1:T(4,128)}, u32[]{:S(2)}, u32[]{:S(2)}) collective-permute-start(f32[4,32,1,128]{3,0,2,1:T(4,128)} %get-tuple-element.155), channel_id=1, source_target_pairs={{4,0},{8,4},{12,8},{16,12},{20,16},{24,20},{28,24},{32,28},{36,32}... | collective-permute-start | bytes 196616 | tf_op jit(solution)/shard_map/ppermute | solution.py:17
  897.2 75.2 %collective-permute-start.23 = (f32[4,32,1,128]{3,0,2,1:T(4,128)}, f32[4,32,1,128]{3,0,2,1:T(4,128)}, u32[]{:S(2)}, u32[]{:S(2)}) collective-permute-start(f32[4,32,1,128]{3,0,2,1:T(4,128)} %get-tuple-element.154), channel_id=1, source_target_pairs={{0,4},{4,8},{8,12},{12,16},{16,20},{20,24},{24,28},{28,32},{32,36}... | collective-permute-start | bytes 196616 | tf_op jit(solution)/shard_map/ppermute | solution.py:16
  898.1 7.2 collective-permute-start.20
  902.4 5.6 collective-permute-start.22
  904.9 8.0 collective-permute-start.21
  921.1 43.3 %copy-start.7 = (f32[4,32,16,1]{3,0,2,1:T(4,128)S(1)}, f32[4,32,16,1]{3,0,2,1:T(4,128)}, u32[]{:S(2)}) copy-start(f32[4,32,16,1]{3,0,2,1:T(4,128)} %get-tuple-element.199) | copy-start | bytes 24580
  921.1 43.3 %copy-start.13 = (f32[4,32,16,128]{3,0,2,1:T(4,128)S(1)}, f32[4,32,16,128]{3,0,2,1:T(4,128)}, u32[]{:S(2)}) copy-start(f32[4,32,16,128]{3,0,2,1:T(4,128)} %get-tuple-element.150) | copy-start | bytes 3145732
where the time goes:
time: 989 us; the launch traced here: 979 us
  local copies, waits for them, and re-layouts  481 us (49%)
  other arithmetic  217 us (22%)
  blocking collectives  158 us (16%)
  starting transfers between devices  96.8 us (10%)
  matrix products  20.6 us (2%)
    scatter x5, local copies, waits for them, and re-layouts, neighbours(): south.at[:, :, :, -1]  185 us
    gather x1, local copies, waits for them, and re-layouts, on_device(): forcing = weights * (flat_state[cells] - values)  181 us
    scatter-add x1, other arithmetic, on_device(): lam = jnp.zeros_like(flat_state).at[cells].add(forcing).reshape(x.shape)  171 us
    all_gather x1, blocking collectives, on_device(): arrived = lax.all_gather(payload, 'lon', axis=1, tiled=True)  158 us
    ppermute x10, starting transfers between devices, extended(): before = lax.ppermute(last, axis, up)  51.3 us
    scatter x5, local copies, waits for them, and re-layouts, neighbours(): north.at[:, :, :, 0]  36.8 us
    ppermute x10, starting transfers between devices, extended(): after = lax.ppermute(initial, axis, down)  30 us
  transfers between devices with their start and end apart: 25, of which 2 were waited for; matrix products, arithmetic and copies ran while one was open for 34% of the time, Pallas kernels for 0%

commit v1 on v0

--- a/solution.py
+++ b/solution.py
@@ -4,6 +4,15 @@
 from jax.sharding import PartitionSpec as P
 
 STEPS = 2
+
+
+def _compute_wires(my_data, at_axis):
+    leaves = []
+    for _ in range(lax.axis_size("lon")):
+        leaves.append(my_data)
+    w2 = lax.all_to_all(jnp.stack(leaves), "lon", 0, 0)
+    d_next = jnp.concatenate(w2, axis=at_axis)
+    return d_next
 
 
 def extended(array, sides, width, wrap):
@@ -71,7 +80,7 @@
     weight = jnp.where(valid, obs_weight[0], 0.0)
     cell_float = obs_cell[0].astype(jnp.float32)
     payload = jnp.stack([obs_value[0], weight, cell_float, band.astype(jnp.float32)])
-    arrived = lax.all_gather(payload, "lon", axis=1, tiled=True)
+    arrived = _compute_wires(payload, 1)
     owned = (arrived[3] == lax.axis_index("lon").astype(jnp.float32)).astype(jnp.float32)
     values = arrived[0]
     weights = arrived[1] * owned

time: 989 us -> 811 us (0.82)
  blocking collectives: 158 us -> 0 us
  local copies, waits for them, and re-layouts: 481 us -> 468 us
    all_gather x1 -> x0, blocking collectives: 158 us -> none  [on_device(): arrived = lax.all_gather(payload, 'lon', axis=1, tiled=True)]
    ppermute x10, starting transfers between devices: 51.3 us -> 24 us  [extended(): before = lax.ppermute(last, axis, up)]
    all_to_all x0 -> x1, starting transfers between devices: none -> 14 us  [_compute_wires(): w2 = lax.all_to_all(jnp.stack(leaves), 'lon', 0, 0)]
  transfers between devices with their start and end apart: 25 -> 26, of which waited for: 2 -> 2; matrix products, arithmetic and copies ran while one was open for 34% -> 41% of each run, Pallas kernels for 0% -> 0%
where the time goes in v1:
time: 811 us; the launch traced here: 801 us
  local copies, waits for them, and re-layouts  468 us (58%)
  other arithmetic  216 us (27%)
  starting transfers between devices  94.6 us (12%)
  matrix products  19.5 us (2%)
    scatter x5, local copies, waits for them, and re-layouts, neighbours(): south.at[:, :, :, -1]  185 us
    gather x1, local copies, waits for them, and re-layouts, on_device(): forcing = weights * (flat_state[cells] - values)  181 us
    scatter-add x1, other arithmetic, on_device(): lam = jnp.zeros_like(flat_state).at[cells].add(forcing).reshape(x.shape)  171 us
    ppermute x10, starting transfers between devices, extended(): after = lax.ppermute(initial, axis, down)  38.2 us
    scatter x5, local copies, waits for them, and re-layouts, neighbours(): north.at[:, :, :, 0]  36.8 us
    ppermute x10, starting transfers between devices, extended(): before = lax.ppermute(last, axis, up)  24 us
    ppermute x5, starting transfers between devices, passed_along(): return lax.ppermute(value, axis, pairs)  18.4 us
    concatenate x5, other arithmetic, extended(): array = jnp.concatenate([before, array, after], axis=dim)  17.3 us
  transfers between devices with their start and end apart: 26, of which 2 were waited for; matrix products, arithmetic and copies ran while one was open for 41% of the time, Pallas kernels for 0%

profile of v1, /device:TPU:1, one launch (start us, length us, event | category | flops | bytes accessed | tf_op | source)
XLA Modules:
  0.0 801.4 jit_solution(15531496562600123826)
XLA Ops:
  0.6 2.0 fusion.36
  2.6 3.6 collective-permute-start.16
  6.2 2.0 fusion.41
  8.6 3.1 collective-permute-start
  12.3 2.0 collective-permute-start.2
  16.0 14.0 %all-to-all-start = ((f32[64,4,512]{2,1,0:T(4,128)}), f32[64,4,512]{2,1,0:T(4,128)}, u32[]{:S(2)}, u32[]{:S(2)}) async-start(f32[64,4,512]{2,1,0:T(4,128)} %stack.17), calls=%async_computation | async-start | bytes 1048576 | tf_op jit(solution)/shard_map/all_to_all | solution.py:13
  33.1 3.3 collective-permute-start.10
  36.9 1.9 collective-permute-start.14
  42.6 7.9 collective-permute-start.18
  50.5 1.9 copy.691
  52.5 1.9 copy.698
  54.4 4.6 pad_maximum_fusion.17
  59.0 3.0 collective-permute-start.3
  63.4 11.2 %collective-permute-start.1 = (f32[2,4,32,16]{2,3,1,0:T(8,128)S(1)}, f32[2,4,32,16]{2,3,1,0:T(8,128)S(1)}, u32[]{:S(2)}, u32[]{:S(2)}) collective-permute-start(f32[2,4,32,16]{2,3,1,0:T(8,128)S(1)} %pad_maximum_fusion.20), channel_id=1, source_target_pairs={{0,128},{4,132},{8,136},{12,140},{16,144},{20,148},{24,152},{28,15... | collective-permute-start | bytes 49160 | tf_op jit(solution)/shard_map/ppermute | solution.py:34
  76.1 3.7 pad_maximum_fusion.9
  79.8 1.8 copy.736
  81.7 1.9 copy.726
  83.5 2.6 collective-permute-start.11
  89.8 1.9 copy.735
  94.2 1.9 copy.725
  98.6 4.0 scatter.40
  102.6 3.8 multiply_select_fusion.7
  106.4 12.0 %scatter.44 = f32[4,32,16,128]{3,2,1,0:T(8,128)} dynamic-update-slice(f32[4,32,16,128]{3,2,1,0:T(8,128)} %get-tuple-element.157, f32[4,32,16,1]{3,2,1,0:T(8,128)} %copy.737, s32[]{:T(128)} %constant.234.clone.1, s32[]{:T(128)} %constant.234.clone.1, s32[]{:T(128)} %constant.234.clone.1, s32[]{:T(128)} %constant.236.clone.1) | dynamic-update-slice | bytes 16388 | tf_op jit(solution)/shard_map/scatter | solution.py:49
  118.3 2.0 fusion.31
  120.4 43.3 %scatter.35 = f32[4,32,16,128]{3,0,2,1:T(4,128)} dynamic-update-slice(f32[4,32,16,128]{3,0,2,1:T(4,128)} %get-tuple-element.182, f32[4,32,16,1]{3,0,2,1:T(4,128)S(1)} %copy-done.6, s32[]{:T(128)} %constant.234.clone.1, s32[]{:T(128)} %constant.234.clone.1, s32[]{:T(128)} %constant.234.clone.1, s32[]{:T(128)} %constant.236.clone.1) | dynamic-update-slice | bytes 16388 | tf_op jit(solution)/shard_map/scatter | solution.py:49
  163.7 8.9 %scatter.34 = f32[4,32,16,128]{3,0,2,1:T(4,128)} dynamic-update-slice(f32[4,32,16,128]{3,0,2,1:T(4,128)} %get-tuple-element.181, f32[4,32,16,1]{3,0,2,1:T(4,128)S(1)} %copy-done.5, s32[]{:T(128)} %constant.234.clone.1, s32[]{:T(128)} %constant.234.clone.1, s32[]{:T(128)} %constant.234.clone.1, s32[]{:T(128)} %constant.234.clone.1) | dynamic-update-slice | bytes 16388 | tf_op jit(solution)/shard_map/scatter | solution.py:48
  173.2 2.0 fusion.30
  175.2 5.2 multiply_subtract_fusion.3
  181.7 4.3 collective-permute-start.9
  186.7 5.0 collective-permute-start.5
  192.4 1.9 collective-permute-start.7
  197.8 1.9 copy.715
  199.7 3.0 pad_maximum_fusion.13
  203.5 1.8 copy.712
  205.3 1.8 copy.716
  207.2 3.8 multiply_select_fusion.5
  210.9 43.3 %scatter.39 = f32[4,32,16,128]{3,0,2,1:T(4,128)} dynamic-update-slice(f32[4,32,16,128]{3,0,2,1:T(4,128)} %get-tuple-element.176, f32[4,32,16,1]{3,0,2,1:T(4,128)} %get-tuple-element.205, s32[]{:T(128)} %constant.234.clone.1, s32[]{:T(128)} %constant.234.clone.1, s32[]{:T(128)} %constant.234.clone.1, s32[]{:T(128)} %constant.236.clone.1) | dynamic-update-slice | bytes 16388 | tf_op jit(solution)/shard_map/scatter | solution.py:49
  254.3 8.0 scatter.36
  263.2 4.8 multiply_subtract_fusion.2
  268.1 2.4 fusion.43
  270.7 180.5 %gather_fusion = f32[32768]{0:T(1024)S(1)} fusion(f32[262144]{0:T(1024)S(1)} %bitcast.97, s32[32768]{0:T(1024)S(1)} %broadcast_clamp_fusion), kind=kCustom, calls=%fused_computation | custom fusion | bytes 393216 | tf_op jit(solution)/shard_map/gather | solution.py:89
  451.3 171.5 %scatter_custom_fusion = f32[262144]{0:T(1024)S(1)} fusion(s32[32768]{0:T(1024)S(1)} %bitcast.107, f32[32768]{0:T(1024)S(1)} %subtract_multiply_fusion, f32[]{:T(128)} %constant.239.clone.1), kind=kCustom, calls=%fused_computation.65 | custom fusion | flops 32768 | bytes 1048580 | tf_op jit(solution)/shard_map/scatter-add | solution.py:90
  625.0 8.0 %collective-permute-start.19 = (f32[4,32,1,128]{3,0,2,1:T(4,128)}, f32[4,32,1,128]{3,0,2,1:T(4,128)}, u32[]{:S(2)}, u32[]{:S(2)}) collective-permute-start(f32[4,32,1,128]{3,0,2,1:T(4,128)} %get-tuple-element.174), channel_id=1, source_target_pairs={{4,0},{8,4},{12,8},{16,12},{20,16},{24,20},{28,24},{32,28},{36,32}... | collective-permute-start | bytes 196616 | tf_op jit(solution)/shard_map/ppermute | solution.py:26
  633.7 3.0 collective-permute-start.12
  637.4 1.9 collective-permute-start.15
  642.9 1.9 copy.739
  644.8 3.0 pad_maximum_fusion.8
  647.8 1.8 copy.732
  649.6 1.8 copy.740
  651.5 3.8 multiply_select_fusion.3
  655.3 43.3 %scatter.45 = f32[4,32,16,128]{3,0,2,1:T(4,128)} dynamic-update-slice(f32[4,32,16,128]{3,0,2,1:T(4,128)} %get-tuple-element.170, f32[4,32,16,1]{3,0,2,1:T(4,128)} %get-tuple-element.203, s32[]{:T(128)} %constant.234.clone.1, s32[]{:T(128)} %constant.234.clone.1, s32[]{:T(128)} %constant.234.clone.1, s32[]{:T(128)} %constant.236.clone.1) | dynamic-update-slice | bytes 16388 | tf_op jit(solution)/shard_map/scatter | solution.py:49
  698.6 8.0 scatter.41
  706.6 4.9 fusion.12
  712.9 8.2 %collective-permute-start.24 = (f32[4,32,1,128]{3,0,2,1:T(4,128)}, f32[4,32,1,128]{3,0,2,1:T(4,128)}, u32[]{:S(2)}, u32[]{:S(2)}) collective-permute-start(f32[4,32,1,128]{3,0,2,1:T(4,128)} %get-tuple-element.155), channel_id=1, source_target_pairs={{4,0},{8,4},{12,8},{16,12},{20,16},{24,20},{28,24},{32,28},{36,32}... | collective-permute-start | bytes 196616 | tf_op jit(solution)/shard_map/ppermute | solution.py:26
  721.9 2.9 collective-permute-start.20
  725.5 1.9 collective-permute-start.22
  730.9 1.9 copy.750
  732.8 3.0 pad_maximum_fusion.3
  736.6 1.8 copy.747
  738.4 1.8 copy.751
  740.2 3.8 multiply_select_fusion.1
  744.0 43.3 %scatter.49 = f32[4,32,16,128]{3,0,2,1:T(4,128)} dynamic-update-slice(f32[4,32,16,128]{3,0,2,1:T(4,128)} %get-tuple-element.151, f32[4,32,16,1]{3,0,2,1:T(4,128)} %get-tuple-element.201, s32[]{:T(128)} %constant.234.clone.1, s32[]{:T(128)} %constant.234.clone.1, s32[]{:T(128)} %constant.234.clone.1, s32[]{:T(128)} %constant.236.clone.1) | dynamic-update-slice | bytes 16388 | tf_op jit(solution)/shard_map/scatter | solution.py:49
  787.3 8.0 scatter.46
  795.3 4.6 fusion.7
  (149 shorter events, 45.0 us)
Async XLA Ops:
  2.6 170.0 %collective-permute-start.16 = (f32[4,32,1,128]{3,2,1,0:T(1,128)}, f32[4,32,1,128]{3,2,1,0:T(1,128)S(1)}, u32[]{:S(2)}, u32[]{:S(2)}) collective-permute-start(f32[4,32,1,128]{3,2,1,0:T(1,128)} %get-tuple-element.167), channel_id=1, source_target_pairs={{0,4},{4,8},{8,12},{12,16},{16,20},{20,24},{24,28},{28,32},{32,36}... | collective-permute-start | bytes 196616 | tf_op jit(solution)/shard_map/ppermute | solution.py:25
  8.6 34.0 %collective-permute-start = (f32[4,32,16,1]{1,2,3,0:T(8,128)S(1)}, f32[4,32,16,1]{1,2,3,0:T(8,128)}, u32[]{:S(2)}, u32[]{:S(2)}) collective-permute-start(f32[4,32,16,1]{1,2,3,0:T(8,128)S(1)} %copy.767), channel_id=1, source_target_pairs={{0,1},{1,2},{2,3},{4,5},{5,6},{6,7},{8,9},{9,10},{10,11},{12,13},{... | collective-permute-start | bytes 24584 | tf_op jit(solution)/shard_map/ppermute | solution.py:25
  11.7 2.6 copy-start.27
  11.7 2.6 copy-start.28
  11.7 3.3 copy-start.29
  11.7 3.3 copy-start.30
  12.3 17.7 %copy-start.1 = (f32[4,32,16,128]{3,2,1,0:T(8,128)S(1)}, f32[4,32,16,128]{3,2,1,0:T(8,128)}, u32[]{:S(2)}) copy-start(f32[4,32,16,128]{3,2,1,0:T(8,128)} %param.30) | copy-start | bytes 3145732
  12.3 40.1 %collective-permute-start.2 = (f32[4,32,16,1]{1,2,3,0:T(8,128)S(1)}, f32[4,32,16,1]{1,2,3,0:T(8,128)}, u32[]{:S(2)}, u32[]{:S(2)}) collective-permute-start(f32[4,32,16,1]{1,2,3,0:T(8,128)S(1)} %copy.768), channel_id=1, source_target_pairs={{1,0},{2,1},{3,2},{5,4},{6,5},{7,6},{9,8},{10,9},{11,10},{13,12},{... | collective-permute-start | bytes 24584 | tf_op jit(solution)/shard_map/ppermute | solution.py:26
  16.0 252.2 %all-to-all-start = ((f32[64,4,512]{2,1,0:T(4,128)}), f32[64,4,512]{2,1,0:T(4,128)}, u32[]{:S(2)}, u32[]{:S(2)}) async-start(f32[64,4,512]{2,1,0:T(4,128)} %stack.17), calls=%async_computation | async-start | bytes 1048576 | tf_op jit(solution)/shard_map/all_to_all | solution.py:13
  31.3 7.5 copy-start.2
  33.1 25.9 %collective-permute-start.10 = (f32[4,32,16,1]{1,2,3,0:T(8,128)S(1)}, f32[4,32,16,1]{1,2,3,0:T(8,128)S(1)}, u32[]{:S(2)}, u32[]{:S(2)}) collective-permute-start(f32[4,32,16,1]{1,2,3,0:T(8,128)S(1)} %copy.769), channel_id=1, source_target_pairs={{0,1},{1,2},{2,3},{4,5},{5,6},{6,7},{8,9},{9,10},{10,11},{12,13},{... | collective-permute-start | bytes 24584 | tf_op jit(solution)/shard_map/ppermute | solution.py:25
  36.9 26.5 %collective-permute-start.14 = (f32[4,32,16,1]{1,2,3,0:T(8,128)S(1)}, f32[4,32,16,1]{1,2,3,0:T(8,128)S(1)}, u32[]{:S(2)}, u32[]{:S(2)}) collective-permute-start(f32[4,32,16,1]{1,2,3,0:T(8,128)S(1)} %copy.770), channel_id=1, source_target_pairs={{1,0},{2,1},{3,2},{5,4},{6,5},{7,6},{9,8},{10,9},{11,10},{13,12},{... | collective-permute-start | bytes 24584 | tf_op jit(solution)/shard_map/ppermute | solution.py:26
  39.5 1.0 copy-start.3
  41.2 0.7 copy-start.26
  42.6 130.6 %collective-permute-start.18 = (f32[4,32,1,128]{3,2,1,0:T(1,128)}, f32[4,32,1,128]{3,2,1,0:T(1,128)}, u32[]{:S(2)}, u32[]{:S(2)}) collective-permute-start(f32[4,32,1,128]{3,2,1,0:T(1,128)} %get-tuple-element.168), channel_id=1, source_target_pairs={{4,0},{8,4},{12,8},{16,12},{20,16},{24,20},{28,24},{32,28},{36,32}... | collective-permute-start | bytes 196616 | tf_op jit(solution)/shard_map/ppermute | solution.py:26
  52.4 122.8 %collective-permute-start.4 = (f32[4,32,1,128]{3,0,2,1:T(4,128)}, f32[4,32,1,128]{3,0,2,1:T(4,128)}, u32[]{:S(2)}, u32[]{:S(2)}) collective-permute-start(f32[4,32,1,128]{3,0,2,1:T(4,128)} %get-tuple-element.186), channel_id=1, source_target_pairs={{4,0},{8,4},{12,8},{16,12},{20,16},{24,20},{28,24},{32,28},{36,32}... | collective-permute-start | bytes 196616 | tf_op jit(solution)/shard_map/ppermute | solution.py:26
  59.0 116.2 %collective-permute-start.3 = (f32[4,32,1,128]{3,0,2,1:T(4,128)}, f32[4,32,1,128]{3,0,2,1:T(4,128)}, u32[]{:S(2)}, u32[]{:S(2)}) collective-permute-start(f32[4,32,1,128]{3,0,2,1:T(4,128)} %get-tuple-element.185), channel_id=1, source_target_pairs={{0,4},{4,8},{8,12},{12,16},{16,20},{20,24},{24,28},{28,32},{32,36}... | collective-permute-start | bytes 196616 | tf_op jit(solution)/shard_map/ppermute | solution.py:25
  63.4 20.1 %collective-permute-start.1 = (f32[2,4,32,16]{2,3,1,0:T(8,128)S(1)}, f32[2,4,32,16]{2,3,1,0:T(8,128)S(1)}, u32[]{:S(2)}, u32[]{:S(2)}) collective-permute-start(f32[2,4,32,16]{2,3,1,0:T(8,128)S(1)} %pad_maximum_fusion.20), channel_id=1, source_target_pairs={{0,128},{4,132},{8,136},{12,140},{16,144},{20,148},{24,152},{28,15... | collective-permute-start | bytes 49160 | tf_op jit(solution)/shard_map/ppermute | solution.py:34
  83.5 6.3 collective-permute-start.11
  98.6 4.0 copy-start.25
  106.4 12.0 %copy-start.10 = (f32[4,32,16,128]{3,2,1,0:T(8,128)S(1)}, f32[4,32,16,128]{3,2,1,0:T(8,128)}, u32[]{:S(2)}) copy-start(f32[4,32,16,128]{3,2,1,0:T(8,128)} %scatter.40) | copy-start | bytes 3145732
  118.3 2.0 copy-start.6
  120.4 43.3 %copy-start.5 = (f32[4,32,16,1]{3,0,2,1:T(4,128)S(1)}, f32[4,32,16,1]{3,0,2,1:T(4,128)}, u32[]{:S(2)}) copy-start(f32[4,32,16,1]{3,0,2,1:T(4,128)} %get-tuple-element.206) | copy-start | bytes 24580
  172.5 2.6 copy-start.4
  172.5 2.7 copy-start.11
  172.5 2.7 copy-start.12
  172.5 2.7 copy-start.23
  172.6 0.6 copy-start.22
  175.1 5.2 copy-start.17
  175.1 5.2 copy-start.18
  175.1 5.2 copy-start.19
  175.1 5.3 copy-start.20
  175.2 5.3 copy-start.21
  181.7 80.5 %collective-permute-start.9 = (f32[4,32,1,128]{3,0,2,1:T(4,128)}, f32[4,32,1,128]{3,0,2,1:T(4,128)}, u32[]{:S(2)}, u32[]{:S(2)}) collective-permute-start(f32[4,32,1,128]{3,0,2,1:T(4,128)} %get-tuple-element.180), channel_id=1, source_target_pairs={{4,0},{8,4},{12,8},{16,12},{20,16},{24,20},{28,24},{32,28},{36,32}... | collective-permute-start | bytes 196616 | tf_op jit(solution)/shard_map/ppermute | solution.py:26
  186.0 77.2 %collective-permute-start.8 = (f32[4,32,1,128]{3,0,2,1:T(4,128)}, f32[4,32,1,128]{3,0,2,1:T(4,128)}, u32[]{:S(2)}, u32[]{:S(2)}) collective-permute-start(f32[4,32,1,128]{3,0,2,1:T(4,128)} %get-tuple-element.179), channel_id=1, source_target_pairs={{0,4},{4,8},{8,12},{12,16},{16,20},{20,24},{24,28},{28,32},{32,36}... | collective-permute-start | bytes 196616 | tf_op jit(solution)/shard_map/ppermute | solution.py:25
  186.7 9.8 %collective-permute-start.5 = (f32[4,32,16,1]{1,2,3,0:T(8,128)S(1)}, f32[4,32,16,1]{1,2,3,0:T(8,128)S(1)}, u32[]{:S(2)}, u32[]{:S(2)}) collective-permute-start(f32[4,32,16,1]{1,2,3,0:T(8,128)S(1)} %copy.708), channel_id=1, source_target_pairs={{0,1},{1,2},{2,3},{4,5},{5,6},{6,7},{8,9},{9,10},{10,11},{12,13},{... | collective-permute-start | bytes 24584 | tf_op jit(solution)/shard_map/ppermute | solution.py:25
  192.4 5.4 collective-permute-start.7
  194.9 7.8 collective-permute-start.6
  210.9 43.3 %copy-start.8 = (f32[4,32,16,1]{3,0,2,1:T(4,128)S(1)}, f32[4,32,16,1]{3,0,2,1:T(4,128)}, u32[]{:S(2)}) copy-start(f32[4,32,16,1]{3,0,2,1:T(4,128)} %get-tuple-element.204) | copy-start | bytes 24580
  210.9 43.3 %copy-start.14 = (f32[4,32,16,128]{3,0,2,1:T(4,128)S(1)}, f32[4,32,16,128]{3,0,2,1:T(4,128)}, u32[]{:S(2)}) copy-start(f32[4,32,16,128]{3,0,2,1:T(4,128)} %get-tuple-element.175) | copy-start | bytes 3145732
  262.2 1.0 copy-start.15
  268.1 183.1 %copy-start = (f32[4,32,16,128]{3,2,1,0:T(8,128)}, f32[4,32,16,128]{3,2,1,0:T(8,128)S(1)}, u32[]{:S(2)}) copy-start(f32[4,32,16,128]{3,2,1,0:T(8,128)S(1)} %copy.753) | copy-start | bytes 3145732
  625.0 81.6 %collective-permute-start.19 = (f32[4,32,1,128]{3,0,2,1:T(4,128)}, f32[4,32,1,128]{3,0,2,1:T(4,128)}, u32[]{:S(2)}, u32[]{:S(2)}) collective-permute-start(f32[4,32,1,128]{3,0,2,1:T(4,128)} %get-tuple-element.174), channel_id=1, source_target_pairs={{4,0},{8,4},{12,8},{16,12},{20,16},{24,20},{28,24},{32,28},{36,32}... | collective-permute-start | bytes 196616 | tf_op jit(solution)/shard_map/ppermute | solution.py:26
  633.0 73.6 %collective-permute-start.17 = (f32[4,32,1,128]{3,0,2,1:T(4,128)}, f32[4,32,1,128]{3,0,2,1:T(4,128)}, u32[]{:S(2)}, u32[]{:S(2)}) collective-permute-start(f32[4,32,1,128]{3,0,2,1:T(4,128)} %get-tuple-element.173), channel_id=1, source_target_pairs={{0,4},{4,8},{8,12},{12,16},{16,20},{20,24},{24,28},{28,32},{32,36}... | collective-permute-start | bytes 196616 | tf_op jit(solution)/shard_map/ppermute | solution.py:25
  633.7 8.0 collective-permute-start.12
  637.4 5.5 collective-permute-start.15
  639.9 7.8 collective-permute-start.13
  655.3 43.3 %copy-start.9 = (f32[4,32,16,1]{3,0,2,1:T(4,128)S(1)}, f32[4,32,16,1]{3,0,2,1:T(4,128)}, u32[]{:S(2)}) copy-start(f32[4,32,16,1]{3,0,2,1:T(4,128)} %get-tuple-element.202) | copy-start | bytes 24580
  655.3 43.3 %copy-start.16 = (f32[4,32,16,128]{3,0,2,1:T(4,128)S(1)}, f32[4,32,16,128]{3,0,2,1:T(4,128)}, u32[]{:S(2)}) copy-start(f32[4,32,16,128]{3,0,2,1:T(4,128)} %get-tuple-element.169) | copy-start | bytes 3145732
  698.6 8.0 copy-start.24
  712.9 82.4 %collective-permute-start.24 = (f32[4,32,1,128]{3,0,2,1:T(4,128)}, f32[4,32,1,128]{3,0,2,1:T(4,128)}, u32[]{:S(2)}, u32[]{:S(2)}) collective-permute-start(f32[4,32,1,128]{3,0,2,1:T(4,128)} %get-tuple-element.155), channel_id=1, source_target_pairs={{4,0},{8,4},{12,8},{16,12},{20,16},{24,20},{28,24},{32,28},{36,32}... | collective-permute-start | bytes 196616 | tf_op jit(solution)/shard_map/ppermute | solution.py:26
  721.0 74.3 %collective-permute-start.23 = (f32[4,32,1,128]{3,0,2,1:T(4,128)}, f32[4,32,1,128]{3,0,2,1:T(4,128)}, u32[]{:S(2)}, u32[]{:S(2)}) collective-permute-start(f32[4,32,1,128]{3,0,2,1:T(4,128)} %get-tuple-element.154), channel_id=1, source_target_pairs={{0,4},{4,8},{8,12},{12,16},{16,20},{20,24},{24,28},{28,32},{32,36}... | collective-permute-start | bytes 196616 | tf_op jit(solution)/shard_map/ppermute | solution.py:25
  721.9 7.4 collective-permute-start.20
  725.5 5.3 collective-permute-start.22
  728.1 7.7 collective-permute-start.21
  744.0 43.3 %copy-start.7 = (f32[4,32,16,1]{3,0,2,1:T(4,128)S(1)}, f32[4,32,16,1]{3,0,2,1:T(4,128)}, u32[]{:S(2)}) copy-start(f32[4,32,16,1]{3,0,2,1:T(4,128)} %get-tuple-element.200) | copy-start | bytes 24580
  744.0 43.3 %copy-start.13 = (f32[4,32,16,128]{3,0,2,1:T(4,128)S(1)}, f32[4,32,16,128]{3,0,2,1:T(4,128)}, u32[]{:S(2)}) copy-start(f32[4,32,16,128]{3,0,2,1:T(4,128)} %get-tuple-element.150) | copy-start | bytes 3145732
